TPU v7x, 256 devices: a whole 4x4x8 slice. The times are simulated.
256 devices in a mesh: space: 32 (over x, z), dp: 8 (over y, core).
Axes of the slice: x: 4, y: 4, z: 8, core: 2. Of those that a mesh axis runs over, the one named last changes fastest.
Arguments:
- features: bfloat16 [8, 16384, 128], P('dp', 'space'), may hold values from -6 to 6
- cotangent: bfloat16 [8, 16384, 128], P('dp', 'space'), may hold values from -6 to 6
- weight_one: bfloat16 [27, 128, 128], replicated, may hold values from -0.21875 to 0.21875
- weight_two: bfloat16 [27, 128, 128], replicated, may hold values from -0.21875 to 0.21875
- rules: int32 [8, 32, 2, 27, 256], P('dp', 'space'), may hold values from 0 to 1024, as said below
- halo_send: int32 [8, 32, 2, 2], P('dp', 'space'), may hold values from 0 to 3
- block_counts: int32 [8, 128], P('dp', 'space'), may hold values from 16 to 128
Outputs:
- grad_features: float32 [8, 16384, 128], P('dp', 'space')
- grad_one: float32 [27, 128, 128], replicated
- grad_two: float32 [27, 128, 128], replicated
Inputs may be any that keep to these rules, and one draw needn't show every extreme that they name: `rules`: for each scene, slab and offset, the live slots come first and hold distinct targets and distinct sources; padding slots hold source 1024 and target 512; at least half of the slots are live, and offset 13 is full with each source equal to its target.
All inputs are finite; a program needn't handle non-finite values.
Results may differ from a plain program's by a relative error of at most 0.0032.
Values may be sent and summed in bfloat16 or wider, within the bound.
No kernel may reach another device: no remote copies, remote signals or barrier semaphores. Data moves between devices by JAX's collectives and lax.ppermute only.
A program may use at most 64 MiB of HBM per device.

v0:
```python
import jax
import jax.numpy as jnp
from jax import lax
from jax.sharding import PartitionSpec as P


def with_halo(block, sides, width):
    for axis, dim in sides:
        count = lax.axis_size(axis)
        forward = [(i, i + 1) for i in range(count - 1)]
        backward = [(target, source) for source, target in forward]
        low = lax.ppermute(
            lax.slice_in_dim(block, block.shape[dim] - width, None, axis=dim), axis, forward
        )
        high = lax.ppermute(lax.slice_in_dim(block, 0, width, axis=dim), axis, backward)
        block = jnp.concatenate([low, block, high], axis=dim)
    return block


def one_hot_rows(index, count):
    return (index[:, None] == jnp.arange(count, dtype=jnp.int32)[None, :]).astype(jnp.bfloat16)


def lift_rows(selector, table):
    return jnp.dot(selector, table, preferred_element_type=jnp.float32).astype(jnp.bfloat16)


def place_rows(selector, values):
    return jnp.einsum("re,rc->ec", selector, values, preferred_element_type=jnp.float32).astype(
        jnp.bfloat16
    )


def body(features, cotangent, weight_one, weight_two, rules, halo_send, block_counts):
    feats = features[0]
    cot = cotangent[0]
    links = rules[0, 0]
    sends = halo_send[0, 0]
    counts = block_counts[0]
    rows, width = feats.shape
    blocks = counts.shape[0]
    block = rows // blocks
    per_side = sends.shape[1]
    halo_rows = per_side * block
    rule_slots = links.shape[2]
    ext_rows = rows + 2 * halo_rows
    sources = links[0]
    targets = links[1]
    active = (jnp.arange(block)[None, :] < counts[:, None]).astype(jnp.float32).reshape(rows, 1)
    active_half = active.astype(jnp.bfloat16)
    xa = feats * active_half
    ga = cot * active_half
    block_pick = one_hot_rows(sends.reshape(-1), blocks)

    def pick_blocks(table):
        picked = jnp.dot(
            block_pick, table.reshape(blocks, block * width), preferred_element_type=jnp.float32
        )
        return picked.astype(jnp.bfloat16).reshape(2 * halo_rows, width)

    def add_blocks(own, back):
        pieces = jnp.concatenate([back[:halo_rows], back[3 * halo_rows :]], axis=0).reshape(
            2 * per_side, block * width
        )
        added = jnp.einsum(
            "be,bc->ec",
            block_pick.astype(jnp.float32),
            pieces,
            precision=lax.Precision.HIGHEST,
            preferred_element_type=jnp.float32,
        )
        return own + added.reshape(rows, width)

    rim_x = with_halo(pick_blocks(xa), (("space", 0),), halo_rows)
    ext_x = jnp.concatenate([xa, rim_x[:halo_rows], rim_x[3 * halo_rows :]], axis=0)

    def forward_step(total, item):
        src, tgt, weight = item
        placed = place_rows(one_hot_rows(tgt, rows), lift_rows(one_hot_rows(src, ext_rows), ext_x))
        return (total + jnp.dot(placed, weight, preferred_element_type=jnp.float32), None)

    z1, _ = lax.scan(
        forward_step, jnp.zeros((rows, width), jnp.float32), (sources, targets, weight_one)
    )
    y1 = (jax.nn.silu(z1) * active).astype(jnp.bfloat16)
    rim_y = with_halo(pick_blocks(y1), (("space", 0),), halo_rows)
    ext_y = jnp.concatenate([y1, rim_y[:halo_rows], rim_y[3 * halo_rows :]], axis=0)

    def make_backward(table, cot_rows):

        def backward_step(total, item):
            src, tgt, weight = item
            src_pick = one_hot_rows(src, ext_rows)
            cot_picked = lift_rows(one_hot_rows(tgt, rows), cot_rows)
            grad_kernel = jnp.einsum(
                "rc,rd->cd",
                lift_rows(src_pick, table),
                cot_picked,
                preferred_element_type=jnp.float32,
            )
            placed = place_rows(src_pick, cot_picked)
            total = total + jnp.einsum(
                "ed,cd->ec", placed, weight, preferred_element_type=jnp.float32
            )
            return (total, grad_kernel)

        return backward_step

    dext_y, grad_second = lax.scan(
        make_backward(ext_y, ga),
        jnp.zeros((ext_rows, width), jnp.float32),
        (sources, targets, weight_two),
    )
    back_y = with_halo(dext_y[rows:], (("space", 0),), halo_rows)
    dy1 = add_blocks(dext_y[:rows], back_y)
    sig = jax.nn.sigmoid(z1)
    dz1 = (dy1 * sig * (1.0 + z1 * (1.0 - sig)) * active).astype(jnp.bfloat16)
    dext_x, grad_first = lax.scan(
        make_backward(ext_x, dz1),
        jnp.zeros((ext_rows, width), jnp.float32),
        (sources, targets, weight_one),
    )
    back_x = with_halo(dext_x[rows:], (("space", 0),), halo_rows)
    grad_rows = add_blocks(dext_x[:rows], back_x) * active
    total_first, total_second = lax.psum((grad_first, grad_second), ("space", "dp"))
    scale = 1.0 / jnp.sqrt(jnp.float32(lax.axis_size("dp") * lax.axis_size("space") * rule_slots))
    return (grad_rows[None], total_first * scale, total_second * scale)


def solution(mesh):
    in_specs = (
        P("dp", "space", None),
        P("dp", "space", None),
        P(),
        P(),
        P("dp", "space", None, None, None),
        P("dp", "space", None, None),
        P("dp", "space"),
    )
    out_specs = (P("dp", "space", None), P(), P())
    return jax.shard_map(body, mesh=mesh, in_specs=in_specs, out_specs=out_specs, check_vma=False)
```

profile of v0, /device:TPU:97, one launch (start us, length us, event | category | flops | bytes accessed | tf_op | source)
XLA Modules:
  0.0 510.2 jit_solution(6266760315622303141)
XLA Ops:
  10.2 1.9 collective-permute-start.1
  12.2 4.8 collective-permute-start
  19.1 45.4 %while.37 = (s32[]{:T(128)}, f32[512,128]{1,0:T(8,128)S(1)}, s32[27,256]{1,0:T(8,128)S(1)}, s32[27,256]{1,0:T(8,128)S(1)}, bf16[1024,128]{1,0:T(8,128)(2,1)S(1)}...) while((s32[]{:T(128)}, f32[512,128]{1,0:T(8,128)S(1)}, s32[27,256]{1,0:T(8,128)S(1)}, ...), condition=%wide.region_1.2_spmd.clone, body=%wide.region_0.1_spmd.clone.sunk | while | flops 118063104 | bytes 956527 | solution.py:82
  65.2 1.9 collective-permute-start.3
  67.2 4.6 collective-permute-start.2
  73.3 64.6 %while.38 = (s32[]{:T(128)}, f32[1024,128]{1,0:T(8,128)S(1)}, f32[27,128,128]{2,1,0:T(8,128)S(1)}, s32[27,256]{1,0:T(8,128)S(1)}, s32[27,256]{1,0:T(8,128)S(1)},...) while((s32[]{:T(128)}, f32[1024,128]{1,0:T(8,128)S(1)}, ...), condition=%wide.region_3.4_spmd.clone, body=%wide.region_2.3_spmd.clone.sunk | while | flops 210829312 | bytes 1744003 | solution.py:109
  73.6 1.5 convolution_add_fusion.7
  76.0 1.5 convolution_add_fusion.7
  78.4 1.5 convolution_add_fusion.7
  80.8 1.5 convolution_add_fusion.7
  83.2 1.5 convolution_add_fusion.7
  85.6 1.5 convolution_add_fusion.7
  87.9 1.5 convolution_add_fusion.7
  90.3 1.5 convolution_add_fusion.7
  137.9 4.9 collective-permute-start.4
  142.8 1.9 collective-permute-start.5
  144.8 5.1 collective-permute-done.5
  149.8 1.6 pad_maximum_fusion.2
  156.0 64.5 %while.39 = (s32[]{:T(128)}, f32[1024,128]{1,0:T(8,128)S(1)}, f32[27,128,128]{2,1,0:T(8,128)S(1)}, s32[27,256]{1,0:T(8,128)S(1)}, s32[27,256]{1,0:T(8,128)S(1)},...) while((s32[]{:T(128)}, f32[1024,128]{1,0:T(8,128)S(1)}, ...), condition=%wide.region_5.6_spmd.clone, body=%wide.region_4.5_spmd.clone.sunk | while | flops 210829312 | bytes 1744003 | solution.py:118
  221.8 1.9 collective-permute-start.6
  223.7 3.4 collective-permute-start.7
  227.5 3.1 collective-permute-done.7
  232.3 266.6 %all-reduce.3.cloned.1.call-done = (f32[27,128,128]{2,1,0:T(8,128)}, f32[27,128,128]{2,1,0:T(8,128)}) async-done(((f32[27,128,128]{2,1,0:T(8,128)}, f32[27,128,128]{2,1,0:T(8,128)}), (f32[27,128,128]{2,1,0:T(8,128)}, f32[27,128,128]{2,1,0:T(8,128)})) %all-reduce.3.cloned.1.call-update) | async-done | bytes 3538960 | tf_op jit(solution)/shard_map/psum | solution.py:125
  498.9 3.0 broadcast_multiply_fusion.1
  (343 shorter events, 175.9 us)
Async XLA Ops:
  7.2 491.8 %all-reduce.3.cloned.1.call-start = ((), (), s32[]{:S(2)}) async-start(), calls=%async_computation | async-start | bytes 7077888 | tf_op jit(solution)/shard_map/psum | solution.py:125
  10.2 8.8 %collective-permute-start.1 = (bf16[256,128]{1,0:T(8,128)(2,1)S(1)}, bf16[256,128]{1,0:T(8,128)(2,1)S(1)}, u32[]{:S(2)}, u32[]{:S(2)}) collective-permute-start(bf16[256,128]{1,0:T(8,128)(2,1)S(1)} %slice.61), channel_id=1, source_target_pairs={{8,0},{16,8},{24,16},{32,24},{40,32},{48,40},{56,48},{64,56},{72,6... | collective-permute-start | bytes 196616 | tf_op jit(solution)/shard_map/ppermute | solution.py:15
  12.2 6.9 %collective-permute-start = (bf16[256,128]{1,0:T(8,128)(2,1)S(1)}, bf16[256,128]{1,0:T(8,128)(2,1)S(1)}, u32[]{:S(2)}, u32[]{:S(2)}) collective-permute-start(bf16[256,128]{1,0:T(8,128)(2,1)S(1)} %slice.59), channel_id=1, source_target_pairs={{0,8},{8,16},{16,24},{24,32},{32,40},{40,48},{48,56},{56,64},{64,7... | collective-permute-start | bytes 196616 | tf_op jit(solution)/shard_map/ppermute | solution.py:12
  64.5 8.8 %copy-start.3 = (bf16[1024,128]{1,0:T(8,128)(2,1)}, bf16[1024,128]{1,0:T(8,128)(2,1)S(1)}, u32[]{:S(2)}) copy-start(bf16[1024,128]{1,0:T(8,128)(2,1)S(1)} %get-tuple-element.511) | copy-start | bytes 786436
  65.2 6.5 %collective-permute-start.3 = (bf16[256,128]{1,0:T(8,128)(2,1)S(1)}, bf16[256,128]{1,0:T(8,128)(2,1)S(1)}, u32[]{:S(2)}, u32[]{:S(2)}) collective-permute-start(bf16[256,128]{1,0:T(8,128)(2,1)S(1)} %slice.65), channel_id=1, source_target_pairs={{8,0},{16,8},{24,16},{32,24},{40,32},{48,40},{56,48},{64,56},{72,6... | collective-permute-start | bytes 196616 | tf_op jit(solution)/shard_map/ppermute | solution.py:15
  67.2 5.9 %collective-permute-start.2 = (bf16[256,128]{1,0:T(8,128)(2,1)S(1)}, bf16[256,128]{1,0:T(8,128)(2,1)S(1)}, u32[]{:S(2)}, u32[]{:S(2)}) collective-permute-start(bf16[256,128]{1,0:T(8,128)(2,1)S(1)} %slice.63), channel_id=1, source_target_pairs={{0,8},{8,16},{16,24},{24,32},{32,40},{40,48},{48,56},{56,64},{64,7... | collective-permute-start | bytes 196616 | tf_op jit(solution)/shard_map/ppermute | solution.py:12
  137.9 17.0 %copy-start.1 = (f32[27,128,128]{2,1,0:T(8,128)}, f32[27,128,128]{2,1,0:T(8,128)S(1)}, u32[]{:S(2)}) copy-start(f32[27,128,128]{2,1,0:T(8,128)S(1)} %get-tuple-element.125) | copy-start | bytes 5308420
  137.9 6.8 %collective-permute-start.4 = (f32[256,128]{1,0:T(8,128)S(1)}, f32[256,128]{1,0:T(8,128)S(1)}, u32[]{:S(2)}, u32[]{:S(2)}) collective-permute-start(f32[256,128]{1,0:T(8,128)S(1)} %get-tuple-element.255), channel_id=1, source_target_pairs={{0,8},{8,16},{16,24},{24,32},{32,40},{40,48},{48,56},{56,64},{64,7... | collective-permute-start | bytes 393224 | tf_op jit(solution)/shard_map/ppermute | solution.py:12
  142.8 7.0 %collective-permute-start.5 = (f32[256,128]{1,0:T(8,128)S(1)}, f32[256,128]{1,0:T(8,128)}, u32[]{:S(2)}, u32[]{:S(2)}) collective-permute-start(f32[256,128]{1,0:T(8,128)S(1)} %get-tuple-element.256), channel_id=1, source_target_pairs={{8,0},{16,8},{24,16},{32,24},{40,32},{48,40},{56,48},{64,56},{72,6... | collective-permute-start | bytes 393224 | tf_op jit(solution)/shard_map/ppermute | solution.py:15
  155.0 1.0 copy-start.4
  220.5 1.2 copy-start
  221.8 5.7 %collective-permute-start.6 = (f32[256,128]{1,0:T(8,128)S(1)}, f32[256,128]{1,0:T(8,128)S(1)}, u32[]{:S(2)}, u32[]{:S(2)}) collective-permute-start(f32[256,128]{1,0:T(8,128)S(1)} %get-tuple-element.253), channel_id=1, source_target_pairs={{0,8},{8,16},{16,24},{24,32},{32,40},{40,48},{48,56},{56,64},{64,7... | collective-permute-start | bytes 393224 | tf_op jit(solution)/shard_map/ppermute | solution.py:12
  223.7 6.9 %collective-permute-start.7 = (f32[256,128]{1,0:T(8,128)S(1)}, f32[256,128]{1,0:T(8,128)S(1)}, u32[]{:S(2)}, u32[]{:S(2)}) collective-permute-start(f32[256,128]{1,0:T(8,128)S(1)} %get-tuple-element.254), channel_id=1, source_target_pairs={{8,0},{16,8},{24,16},{32,24},{40,32},{48,40},{56,48},{64,56},{72,6... | collective-permute-start | bytes 393224 | tf_op jit(solution)/shard_map/ppermute | solution.py:15
  498.9 3.0 copy-start.2
Sparse Core Ops, SparseCore 0:
  221.9 276.9 all-reduce.2
where the time goes:
time: 516 us; the launch traced here: 510 us
  waiting for transfers between devices  277 us (54%)
  matrix products  173 us (34%)
  starting transfers between devices  25.3 us (5%)
  between operations  14.4 us (3%)
  local copies, waits for them, and re-layouts  9.04 us (2%)
  other arithmetic  9.03 us (2%)
    psum x1, waiting for transfers between devices, body(): lax.psum((grad_first, grad_second), ('space', 'dp'))  267 us
    dot_general x54, matrix products, backward_step(): jnp.einsum('ed,cd->ec', placed, weight, preferred_element_type=jnp.float32)  81.1 us
    dot_general x27, matrix products, forward_step(): jnp.dot(placed, weight, preferred_element_type=jnp.float32)  34.5 us
    dot_general x54, matrix products, backward_step(): jnp.einsum('rc,rd->cd', lift_rows(src_pick, table), cot_picked, preferred...  30.3 us
    dot_general x81, matrix products, lift_rows(): jnp.dot(selector, table, preferred_element_type=jnp.float32)  24.5 us
    ppermute x4, starting transfers between devices, with_halo(): lax.ppermute(lax.slice_in_dim(block, block.shape[dim] - width, None, axis...  16.1 us
  transfers between devices with their start and end apart: 9, of which 5 were waited for; matrix products, arithmetic and copies ran while one was open for 1% of the time, Pallas kernels for 0%

commit v1 on v0

--- a/solution.py
+++ b/solution.py
@@ -19,16 +19,6 @@
 
 def one_hot_rows(index, count):
     return (index[:, None] == jnp.arange(count, dtype=jnp.int32)[None, :]).astype(jnp.bfloat16)
-
-
-def lift_rows(selector, table):
-    return jnp.dot(selector, table, preferred_element_type=jnp.float32).astype(jnp.bfloat16)
-
-
-def place_rows(selector, values):
-    return jnp.einsum("re,rc->ec", selector, values, preferred_element_type=jnp.float32).astype(
-        jnp.bfloat16
-    )
 
 
 def body(features, cotangent, weight_one, weight_two, rules, halo_send, block_counts):
@@ -73,57 +63,37 @@
 
     rim_x = with_halo(pick_blocks(xa), (("space", 0),), halo_rows)
     ext_x = jnp.concatenate([xa, rim_x[:halo_rows], rim_x[3 * halo_rows :]], axis=0)
+    src_pick = (sources[:, :, None] == jnp.arange(ext_rows, dtype=jnp.int32)).astype(jnp.bfloat16)
+    tgt_pick = (targets[:, :, None] == jnp.arange(rows, dtype=jnp.int32)).astype(jnp.bfloat16)
 
-    def forward_step(total, item):
-        src, tgt, weight = item
-        placed = place_rows(one_hot_rows(tgt, rows), lift_rows(one_hot_rows(src, ext_rows), ext_x))
-        return (total + jnp.dot(placed, weight, preferred_element_type=jnp.float32), None)
+    def exact(spec, a, b):
+        return jnp.einsum(spec, a, b, preferred_element_type=jnp.float32).astype(jnp.bfloat16)
 
-    z1, _ = lax.scan(
-        forward_step, jnp.zeros((rows, width), jnp.float32), (sources, targets, weight_one)
-    )
+    gathered = exact("kre,ec->krc", src_pick, ext_x)
+    placed = exact("kro,krc->koc", tgt_pick, gathered)
+    z1 = jnp.einsum("koc,kcd->od", placed, weight_one, preferred_element_type=jnp.float32)
     y1 = (jax.nn.silu(z1) * active).astype(jnp.bfloat16)
     rim_y = with_halo(pick_blocks(y1), (("space", 0),), halo_rows)
     ext_y = jnp.concatenate([y1, rim_y[:halo_rows], rim_y[3 * halo_rows :]], axis=0)
 
-    def make_backward(table, cot_rows):
+    def backward(table, cot_rows, weight):
+        cot_picked = exact("kro,oc->krc", tgt_pick, cot_rows)
+        at_source = exact("kre,krc->kec", src_pick, cot_picked)
+        dext = jnp.einsum("ked,kcd->ec", at_source, weight, preferred_element_type=jnp.float32)
+        grad_kernel = jnp.einsum("ec,ked->kcd", table, at_source, preferred_element_type=jnp.float32)
+        return dext, grad_kernel
 
-        def backward_step(total, item):
-            src, tgt, weight = item
-            src_pick = one_hot_rows(src, ext_rows)
-            cot_picked = lift_rows(one_hot_rows(tgt, rows), cot_rows)
-            grad_kernel = jnp.einsum(
-                "rc,rd->cd",
-                lift_rows(src_pick, table),
-                cot_picked,
-                preferred_element_type=jnp.float32,
-            )
-            placed = place_rows(src_pick, cot_picked)
-            total = total + jnp.einsum(
-                "ed,cd->ec", placed, weight, preferred_element_type=jnp.float32
-            )
-            return (total, grad_kernel)
-
-        return backward_step
-
-    dext_y, grad_second = lax.scan(
-        make_backward(ext_y, ga),
-        jnp.zeros((ext_rows, width), jnp.float32),
-        (sources, targets, weight_two),
-    )
+    scale = 1.0 / jnp.sqrt(jnp.float32(lax.axis_size("dp") * lax.axis_size("space") * rule_slots))
+    dext_y, grad_second = backward(ext_y, ga, weight_two)
+    total_second = lax.psum(grad_second, ("space", "dp"))
     back_y = with_halo(dext_y[rows:], (("space", 0),), halo_rows)
     dy1 = add_blocks(dext_y[:rows], back_y)
     sig = jax.nn.sigmoid(z1)
     dz1 = (dy1 * sig * (1.0 + z1 * (1.0 - sig)) * active).astype(jnp.bfloat16)
-    dext_x, grad_first = lax.scan(
-        make_backward(ext_x, dz1),
-        jnp.zeros((ext_rows, width), jnp.float32),
-        (sources, targets, weight_one),
-    )
+    dext_x, grad_first = backward(ext_x, dz1, weight_one)
     back_x = with_halo(dext_x[rows:], (("space", 0),), halo_rows)
     grad_rows = add_blocks(dext_x[:rows], back_x) * active
-    total_first, total_second = lax.psum((grad_first, grad_second), ("space", "dp"))
-    scale = 1.0 / jnp.sqrt(jnp.float32(lax.axis_size("dp") * lax.axis_size("space") * rule_slots))
+    total_first = lax.psum(grad_first, ("space", "dp"))
     return (grad_rows[None], total_first * scale, total_second * scale)
 
 

time: 516 us -> 396 us (0.77)
  matrix products: 173 us -> 62.8 us
    dot_general x216 -> x8, matrix products: 170 us -> 61.2 us  [the longest x3 31.7 us: exact(): jnp.einsum(spec, a, b, preferred_element_type=jnp.float32)]
    psum x1, waiting for transfers between devices: 267 us -> 276 us  [body(): total_first = lax.psum(grad_first, ('space', 'dp'))]
    ppermute x4, waiting for transfers between devices: 8.22 us -> 0.42 us  [with_halo(): lax.ppermute(lax.slice_in_dim(block, 0, width, axis=dim), axis, backward)]
  transfers between devices with their start and end apart: 9 -> 9, of which waited for: 5 -> 3; matrix products, arithmetic and copies ran while one was open for 1% -> 10% of each run, Pallas kernels for 0% -> 0%
where the time goes in v1:
time: 396 us; the launch traced here: 395 us
  waiting for transfers between devices  278 us (70%)
  matrix products  62.8 us (16%)
  starting transfers between devices  26.8 us (7%)
  between operations  14.3 us (4%)
  local copies, waits for them, and re-layouts  7.81 us (2%)
  other arithmetic  4.95 us (1%)
    psum x1, waiting for transfers between devices, body(): total_first = lax.psum(grad_first, ('space', 'dp'))  276 us
    dot_general x3, matrix products, exact(): jnp.einsum(spec, a, b, preferred_element_type=jnp.float32)  31.7 us
    ppermute x4, starting transfers between devices, with_halo(): lax.ppermute(lax.slice_in_dim(block, block.shape[dim] - width, None, axis...  19.1 us
    dot_general x2, matrix products, backward(): jnp.einsum('ec,ked->kcd', table, at_source, preferred_element_type=jnp.fl...  12.5 us
    dot_general x2, matrix products, backward(): jnp.einsum('ked,kcd->ec', at_source, weight, preferred_element_type=jnp.f...  10.2 us
  transfers between devices with their start and end apart: 9, of which 3 were waited for; matrix products, arithmetic and copies ran while one was open for 10% of the time, Pallas kernels for 0%

profile of v1, /device:TPU:97, one launch (start us, length us, event | category | flops | bytes accessed | tf_op | source)
XLA Modules:
  0.0 395.1 jit_solution(422928272534995133)
XLA Ops:
  7.2 1.0 squeeze.11
  10.3 1.9 collective-permute-start.3
  12.3 4.8 %collective-permute-start.2 = (bf16[256,128]{1,0:T(8,128)(2,1)S(1)}, bf16[256,128]{1,0:T(8,128)(2,1)S(1)}, u32[]{:S(2)}, u32[]{:S(2)}) collective-permute-start(bf16[256,128]{1,0:T(8,128)(2,1)S(1)} %slice.62), channel_id=1, source_target_pairs={{0,8},{8,16},{16,24},{24,32},{32,40},{40,48},{48,56},{56,64},{64,7... | collective-permute-start | bytes 196616 | tf_op jit(solution)/shard_map/ppermute | solution.py:12
  17.1 0.9 fusion.62
  18.0 11.8 %fusion.12 = bf16[27,1024,128]{2,1,0:T(8,128)(2,1)} fusion(s32[27,256]{1,0:T(8,128)S(1)} %get-tuple-element.27, s32[27,256]{1,0:T(8,128)S(1)} %get-tuple-element.26, bf16[1,512,128]{2,1,0:T(8,128)(2,1)} %param.8, bf16[512]{0:T(512)(128)(2,1)S(1)} %get-tuple-element.24), kind=kOutput, calls=%fused_computation.16 | convolution fusion | flops 2733015040 | bytes 7265280 | tf_op jit(solution)/shard_map/kre,krc->kec/dot_general | solution.py:70
  29.9 5.2 %convolution_bitcast_fusion.3 = f32[1024,128]{1,0:T(8,128)S(1)} fusion(bf16[27,1024,128]{2,1,0:T(8,128)(2,1)} %fusion.12, bf16[27,128,128]{2,1,0:T(8,128)(2,1)} %param.10), kind=kOutput, calls=%fused_computation.26 | convolution fusion | flops 905969664 | bytes 8486912 | tf_op jit(solution)/shard_map/ked,kcd->ec/dot_general | solution.py:82
  35.1 1.9 collective-permute-start.1
  37.1 4.8 %collective-permute-start = (f32[256,128]{1,0:T(8,128)S(1)}, f32[256,128]{1,0:T(8,128)S(1)}, u32[]{:S(2)}, u32[]{:S(2)}) collective-permute-start(f32[256,128]{1,0:T(8,128)S(1)} %get-tuple-element.13), channel_id=1, source_target_pairs={{0,8},{8,16},{16,24},{24,32},{32,40},{40,48},{48,56},{56,64},{64,7... | collective-permute-start | bytes 393224 | tf_op jit(solution)/shard_map/ppermute | solution.py:12
  42.0 8.6 %fusion.1 = bf16[27,256,128]{2,1,0:T(8,128)(2,1)} fusion(s32[27,256]{1,0:T(8,128)S(1)} %get-tuple-element.27, bf16[256,128]{1,0:T(8,128)(2,1)S(1)} %collective-permute-done.3, bf16[256,128]{1,0:T(8,128)(2,1)S(1)} %collective-permute-done.2, bf16[512,128]{1,0:T(8,128)(2,1)S(1)} %bitcast_multiply_fusion.2), kind=kOutput, calls=%fused_computation.2 | convolution fusion | flops 1819803648 | bytes 2059264 | tf_op jit(solution)/shard_map/kre,ec->krc/dot_general | solution.py:70
  50.6 6.8 %fusion.20 = f32[512,128]{1,0:T(8,128)S(1)} fusion(bf16[27,128,128]{2,1,0:T(8,128)(2,1)S(1)} %copy-done, s32[27,256]{1,0:T(8,128)S(1)} %get-tuple-element.26, bf16[27,256,128]{2,1,0:T(8,128)(2,1)} %fusion.1), kind=kOutput, calls=%fused_computation.27 | convolution fusion | flops 1364262912 | bytes 2944000 | tf_op jit(solution)/shard_map/koc,kcd->od/dot_general | solution.py:74
  58.3 11.2 %fusion.13 = bf16[27,1024,128]{2,1,0:T(8,128)(2,1)} fusion(s32[27,256]{1,0:T(8,128)S(1)} %get-tuple-element.27, s32[27,256]{1,0:T(8,128)S(1)} %get-tuple-element.26, f32[512,128]{1,0:T(8,128)S(1)} %reshape.70, f32[1024,128]{1,0:T(8,128)S(1)} %convolution_bitcast_fusion.3, f32[512,128]{1,0:T(8,128)S(1)} %fusion.20, f32[512]{0:T(512)S(1)} %get-tuple-element.23), kind=kOutput, calls=%fused_computation.17 | convolution fusion | flops 2733670400 | bytes 7931904 | tf_op jit(solution)/shard_map/kre,krc->kec/dot_general | solution.py:70
  69.5 5.0 %convolution_bitcast_fusion.2 = f32[1024,128]{1,0:T(8,128)S(1)} fusion(bf16[27,1024,128]{2,1,0:T(8,128)(2,1)} %fusion.13, bf16[27,128,128]{2,1,0:T(8,128)(2,1)S(1)} %copy-done), kind=kOutput, calls=%fused_computation.25 | convolution fusion | flops 905969664 | bytes 8486912 | tf_op jit(solution)/shard_map/ked,kcd->ec/dot_general | solution.py:82
  74.6 1.9 collective-permute-start.5
  76.5 4.6 %collective-permute-start.4 = (f32[256,128]{1,0:T(8,128)S(1)}, f32[256,128]{1,0:T(8,128)S(1)}, u32[]{:S(2)}, u32[]{:S(2)}) collective-permute-start(f32[256,128]{1,0:T(8,128)S(1)} %get-tuple-element.11), channel_id=1, source_target_pairs={{0,8},{8,16},{16,24},{24,32},{32,40},{40,48},{48,56},{56,64},{64,7... | collective-permute-start | bytes 393224 | tf_op jit(solution)/shard_map/ppermute | solution.py:12
  81.5 1.5 collective-permute-done.4
  85.2 1.9 collective-permute-start.7
  87.2 5.0 %collective-permute-start.6 = (bf16[256,128]{1,0:T(8,128)(2,1)S(1)}, bf16[256,128]{1,0:T(8,128)(2,1)S(1)}, u32[]{:S(2)}, u32[]{:S(2)}) collective-permute-start(bf16[256,128]{1,0:T(8,128)(2,1)S(1)} %slice.69), channel_id=1, source_target_pairs={{0,8},{8,16},{16,24},{24,32},{32,40},{40,48},{48,56},{56,64},{64,7... | collective-permute-start | bytes 196616 | tf_op jit(solution)/shard_map/ppermute | solution.py:12
  92.2 6.3 %convolution_bitcast_fusion.1 = f32[27,128,128]{1,2,0:T(8,128)} fusion(bf16[27,1024,128]{2,1,0:T(8,128)(2,1)} %fusion.13, bf16[256,128]{1,0:T(8,128)(2,1)S(1)} %collective-permute-done.3, bf16[256,128]{1,0:T(8,128)(2,1)S(1)} %collective-permute-done.2, bf16[512,128]{1,0:T(8,128)(2,1)S(1)} %bitcast_multiply_fusion.2), kind=kOutput, calls=%fused_computation.24 | convolution fusion | flops 906756096 | bytes 9109504 | tf_op jit(solution)/shard_map/ec,ked->kcd/dot_general | solution.py:83
  98.4 6.3 %convolution_bitcast_fusion = f32[27,128,128]{1,2,0:T(8,128)} fusion(bf16[27,1024,128]{2,1,0:T(8,128)(2,1)} %fusion.12, bf16[256,128]{1,0:T(8,128)(2,1)S(1)} %collective-permute-done.7, bf16[256,128]{1,0:T(8,128)(2,1)S(1)} %collective-permute-done.6, bf16[512,128]{1,0:T(8,128)(2,1)S(1)} %get-tuple-element.21), kind=kOutput, calls=%fused_computation.23 | convolution fusion | flops 906756096 | bytes 9109504 | tf_op jit(solution)/shard_map/ec,ked->kcd/dot_general | solution.py:83
  104.7 276.5 %all-reduce.3.cloned.1.call-done = (f32[27,128,128]{1,2,0:T(8,128)}, f32[27,128,128]{1,2,0:T(8,128)}) async-done(((f32[27,128,128]{1,2,0:T(8,128)}, f32[27,128,128]{1,2,0:T(8,128)}), (f32[27,128,128]{1,2,0:T(8,128)}, f32[27,128,128]{1,2,0:T(8,128)})) %all-reduce.3.cloned.1.call-update) | async-done | bytes 3538960 | tf_op jit(solution)/shard_map/psum | solution.py:96
  381.2 1.6 broadcast_multiply_fusion.1
  382.8 1.9 copy.18
  384.7 1.6 broadcast_multiply_fusion
  386.3 1.9 copy.19
  (38 shorter events, 5.8 us)
Async XLA Ops:
  7.2 43.5 %copy-start = (bf16[27,128,128]{2,1,0:T(8,128)(2,1)S(1)}, bf16[27,128,128]{2,1,0:T(8,128)(2,1)}, u32[]{:S(2)}) copy-start(bf16[27,128,128]{2,1,0:T(8,128)(2,1)} %param.9) | copy-start | bytes 2654212
  7.2 374.0 %all-reduce.3.cloned.1.call-start = ((), (), s32[]{:S(2)}) async-start(), calls=%async_computation | async-start | bytes 7077888 | tf_op jit(solution)/shard_map/psum | solution.py:96
  10.3 31.6 %collective-permute-start.3 = (bf16[256,128]{1,0:T(8,128)(2,1)S(1)}, bf16[256,128]{1,0:T(8,128)(2,1)S(1)}, u32[]{:S(2)}, u32[]{:S(2)}) collective-permute-start(bf16[256,128]{1,0:T(8,128)(2,1)S(1)} %slice.64), channel_id=1, source_target_pairs={{8,0},{16,8},{24,16},{32,24},{40,32},{48,40},{56,48},{64,56},{72,6... | collective-permute-start | bytes 196616 | tf_op jit(solution)/shard_map/ppermute | solution.py:15
  12.3 29.7 %collective-permute-start.2 = (bf16[256,128]{1,0:T(8,128)(2,1)S(1)}, bf16[256,128]{1,0:T(8,128)(2,1)S(1)}, u32[]{:S(2)}, u32[]{:S(2)}) collective-permute-start(bf16[256,128]{1,0:T(8,128)(2,1)S(1)} %slice.62), channel_id=1, source_target_pairs={{0,8},{8,16},{16,24},{24,32},{32,40},{40,48},{48,56},{56,64},{64,7... | collective-permute-start | bytes 196616 | tf_op jit(solution)/shard_map/ppermute | solution.py:12
  29.9 11.9 %copy-start.1 = (bf16[1,512,128]{2,1,0:T(8,128)(2,1)S(1)}, bf16[1,512,128]{2,1,0:T(8,128)(2,1)}, u32[]{:S(2)}) copy-start(bf16[1,512,128]{2,1,0:T(8,128)(2,1)} %param.7) | copy-start | bytes 393220
  35.1 22.4 %collective-permute-start.1 = (f32[256,128]{1,0:T(8,128)S(1)}, f32[256,128]{1,0:T(8,128)S(1)}, u32[]{:S(2)}, u32[]{:S(2)}) collective-permute-start(f32[256,128]{1,0:T(8,128)S(1)} %get-tuple-element.14), channel_id=1, source_target_pairs={{8,0},{16,8},{24,16},{32,24},{40,32},{48,40},{56,48},{64,56},{72,6... | collective-permute-start | bytes 393224 | tf_op jit(solution)/shard_map/ppermute | solution.py:15
  37.1 20.4 %collective-permute-start = (f32[256,128]{1,0:T(8,128)S(1)}, f32[256,128]{1,0:T(8,128)S(1)}, u32[]{:S(2)}, u32[]{:S(2)}) collective-permute-start(f32[256,128]{1,0:T(8,128)S(1)} %get-tuple-element.13), channel_id=1, source_target_pairs={{0,8},{8,16},{16,24},{24,32},{32,40},{40,48},{48,56},{56,64},{64,7... | collective-permute-start | bytes 393224 | tf_op jit(solution)/shard_map/ppermute | solution.py:12
  74.6 6.9 %collective-permute-start.5 = (f32[256,128]{1,0:T(8,128)S(1)}, f32[256,128]{1,0:T(8,128)S(1)}, u32[]{:S(2)}, u32[]{:S(2)}) collective-permute-start(f32[256,128]{1,0:T(8,128)S(1)} %get-tuple-element.12), channel_id=1, source_target_pairs={{8,0},{16,8},{24,16},{32,24},{40,32},{48,40},{56,48},{64,56},{72,6... | collective-permute-start | bytes 393224 | tf_op jit(solution)/shard_map/ppermute | solution.py:15
  76.5 6.5 %collective-permute-start.4 = (f32[256,128]{1,0:T(8,128)S(1)}, f32[256,128]{1,0:T(8,128)S(1)}, u32[]{:S(2)}, u32[]{:S(2)}) collective-permute-start(f32[256,128]{1,0:T(8,128)S(1)} %get-tuple-element.11), channel_id=1, source_target_pairs={{0,8},{8,16},{16,24},{24,32},{32,40},{40,48},{48,56},{56,64},{64,7... | collective-permute-start | bytes 393224 | tf_op jit(solution)/shard_map/ppermute | solution.py:12
  85.2 13.3 %collective-permute-start.7 = (bf16[256,128]{1,0:T(8,128)(2,1)S(1)}, bf16[256,128]{1,0:T(8,128)(2,1)S(1)}, u32[]{:S(2)}, u32[]{:S(2)}) collective-permute-start(bf16[256,128]{1,0:T(8,128)(2,1)S(1)} %slice.71), channel_id=1, source_target_pairs={{8,0},{16,8},{24,16},{32,24},{40,32},{48,40},{56,48},{64,56},{72,6... | collective-permute-start | bytes 196616 | tf_op jit(solution)/shard_map/ppermute | solution.py:15
  87.2 11.3 %collective-permute-start.6 = (bf16[256,128]{1,0:T(8,128)(2,1)S(1)}, bf16[256,128]{1,0:T(8,128)(2,1)S(1)}, u32[]{:S(2)}, u32[]{:S(2)}) collective-permute-start(bf16[256,128]{1,0:T(8,128)(2,1)S(1)} %slice.69), channel_id=1, source_target_pairs={{0,8},{8,16},{16,24},{24,32},{32,40},{40,48},{48,56},{56,64},{64,7... | collective-permute-start | bytes 196616 | tf_op jit(solution)/shard_map/ppermute | solution.py:12
Sparse Core Ops, SparseCore 0:
  104.8 276.2 all-reduce.2

commit v2 on v1

--- a/solution.py
+++ b/solution.py
@@ -19,6 +19,38 @@
 
 def one_hot_rows(index, count):
     return (index[:, None] == jnp.arange(count, dtype=jnp.int32)[None, :]).astype(jnp.bfloat16)
+
+
+def halve(values, axis, bit):
+    count = lax.axis_size(axis)
+    upper = ((lax.axis_index(axis) >> bit) & 1) == 1
+    pairs = [(i, i ^ (1 << bit)) for i in range(count)]
+    half = values.shape[0] // 2
+    low, high = values[:half], values[half:]
+    return jnp.where(upper, high, low) + lax.ppermute(jnp.where(upper, low, high), axis, pairs)
+
+
+def double(values, axis, bit):
+    count = lax.axis_size(axis)
+    upper = ((lax.axis_index(axis) >> bit) & 1) == 1
+    pairs = [(i, i ^ (1 << bit)) for i in range(count)]
+    got = lax.ppermute(values, axis, pairs)
+    return jnp.where(upper, jnp.concatenate([got, values]), jnp.concatenate([values, got]))
+
+
+def tree_sum(total):
+    parts = lax.axis_size("space")
+    inner = [("dp", 1), ("dp", 2)]
+    values = halve(total, "dp", 0)
+    spread = values.reshape(parts, values.shape[0] // parts, values.shape[1])
+    values = jnp.sum(lax.all_to_all(spread, "space", 0, 0, tiled=True), axis=0)
+    for axis, bit in inner:
+        values = halve(values, axis, bit)
+    for axis, bit in reversed(inner):
+        values = double(values, axis, bit)
+    copies = jnp.broadcast_to(values[None], (parts,) + values.shape)
+    values = lax.all_to_all(copies, "space", 0, 0, tiled=True).reshape(-1, values.shape[1])
+    return double(values, "dp", 0)
 
 
 def body(features, cotangent, weight_one, weight_two, rules, halo_send, block_counts):
@@ -85,7 +117,6 @@
 
     scale = 1.0 / jnp.sqrt(jnp.float32(lax.axis_size("dp") * lax.axis_size("space") * rule_slots))
     dext_y, grad_second = backward(ext_y, ga, weight_two)
-    total_second = lax.psum(grad_second, ("space", "dp"))
     back_y = with_halo(dext_y[rows:], (("space", 0),), halo_rows)
     dy1 = add_blocks(dext_y[:rows], back_y)
     sig = jax.nn.sigmoid(z1)
@@ -93,7 +124,8 @@
     dext_x, grad_first = backward(ext_x, dz1, weight_one)
     back_x = with_halo(dext_x[rows:], (("space", 0),), halo_rows)
     grad_rows = add_blocks(dext_x[:rows], back_x) * active
-    total_first = lax.psum(grad_first, ("space", "dp"))
+    kernels = jnp.concatenate([grad_first, grad_second], axis=0).reshape(-1, width)
+    total_first, total_second = jnp.split(tree_sum(kernels).reshape(-1, width, width), 2, axis=0)
     return (grad_rows[None], total_first * scale, total_second * scale)
 
 

time: 396 us -> 234 us (0.59)
  waiting for transfers between devices: 278 us -> 57.5 us
  blocking collectives: 0 us -> 44.9 us
  starting transfers between devices: 26.8 us -> 58.5 us
  between operations: 14.3 us -> 1.04 us
  matrix products: 62.8 us -> 53.7 us
    psum x1 -> x0, waiting for transfers between devices: 276 us -> none  [body(): total_first = lax.psum(grad_first, ('space', 'dp'))]
    all_to_all x0 -> x1, blocking collectives: none -> 44.9 us  [tree_sum(): lax.all_to_all(copies, 'space', 0, 0, tiled=True)]
    all_to_all x0 -> x1, waiting for transfers between devices: none -> 43.6 us  [tree_sum(): values = jnp.sum(lax.all_to_all(spread, 'space', 0, 0, tiled=True), axis=0)]
    ppermute x0 -> x6, starting transfers between devices: none -> 19.8 us  [the longest x3 11.9 us: double(): got = lax.ppermute(values, axis, pairs)]
    ppermute x0 -> x6, waiting for transfers between devices: none -> 12 us  [the longest x3 6.12 us: double(): got = lax.ppermute(values, axis, pairs)]
    all_to_all x0 -> x1, starting transfers between devices: none -> 12 us  [tree_sum(): values = jnp.sum(lax.all_to_all(spread, 'space', 0, 0, tiled=True), axis=0)]
    dot_general x3, matrix products: 31.7 us -> 26.8 us  [exact(): jnp.einsum(spec, a, b, preferred_element_type=jnp.float32)]
    dot_general x2, matrix products: 12.5 us -> 8.44 us  [backward(): jnp.einsum('ec,ked->kcd', table, at_source, preferred_element_type=jnp.fl...]
  transfers between devices with their start and end apart: 9 -> 15, of which waited for: 3 -> 9; matrix products, arithmetic and copies ran while one was open for 10% -> 15% of each run, Pallas kernels for 0% -> 0%
where the time goes in v2:
time: 234 us; the launch traced here: 230 us
  starting transfers between devices  58.5 us (25%)
  waiting for transfers between devices  57.5 us (25%)
  matrix products  53.7 us (23%)
  blocking collectives  44.9 us (19%)
  local copies, waits for them, and re-layouts  8.13 us (3%)
  other arithmetic  6.45 us (3%)
    all_to_all x1, blocking collectives, tree_sum(): lax.all_to_all(copies, 'space', 0, 0, tiled=True)  44.9 us
    all_to_all x1, waiting for transfers between devices, tree_sum(): values = jnp.sum(lax.all_to_all(spread, 'space', 0, 0, tiled=True), axis=0)  43.6 us
    dot_general x3, matrix products, exact(): jnp.einsum(spec, a, b, preferred_element_type=jnp.float32)  26.8 us
    ppermute x4, starting transfers between devices, with_halo(): lax.ppermute(lax.slice_in_dim(block, block.shape[dim] - width, None, axis...  19.1 us
    all_to_all x1, starting transfers between devices, tree_sum(): values = jnp.sum(lax.all_to_all(spread, 'space', 0, 0, tiled=True), axis=0)  12 us
    ppermute x3, starting transfers between devices, double(): got = lax.ppermute(values, axis, pairs)  11.9 us
    dot_general x2, matrix products, backward(): jnp.einsum('ked,kcd->ec', at_source, weight, preferred_element_type=jnp.f...  10 us
    dot_general x2, matrix products, backward(): jnp.einsum('ec,ked->kcd', table, at_source, preferred_element_type=jnp.fl...  8.44 us
  transfers between devices with their start and end apart: 15, of which 9 were waited for; matrix products, arithmetic and copies ran while one was open for 15% of the time, Pallas kernels for 0%

profile of v2, /device:TPU:97, one launch (start us, length us, event | category | flops | bytes accessed | tf_op | source)
XLA Modules:
  0.0 230.3 jit_solution(8969259852059742881)
XLA Ops:
  3.9 1.9 collective-permute-start.3
  6.0 4.8 %collective-permute-start.2 = (bf16[256,128]{0,1:T(8,128)(2,1)S(1)}, bf16[256,128]{0,1:T(8,128)(2,1)S(1)}, u32[]{:S(2)}, u32[]{:S(2)}) collective-permute-start(bf16[256,128]{0,1:T(8,128)(2,1)S(1)} %copy.19), channel_id=1, source_target_pairs={{0,8},{8,16},{16,24},{24,32},{32,40},{40,48},{48,56},{56,64},{64,7... | collective-permute-start | bytes 196616 | tf_op jit(solution)/shard_map/ppermute | solution.py:12
  12.7 10.7 %fusion.14 = bf16[27,1024,128]{2,1,0:T(8,128)(2,1)} fusion(s32[27,256]{1,0:T(8,128)S(1)} %get-tuple-element.23, s32[27,256]{1,0:T(8,128)S(1)} %get-tuple-element.22, bf16[1,512,128]{1,2,0:T(8,128)(2,1)S(1)} %copy.17, bf16[512]{0:T(512)(128)(2,1)S(1)} %get-tuple-element.20), kind=kOutput, calls=%fused_computation.17 | convolution fusion | flops 2733015040 | bytes 7265280 | tf_op jit(solution)/shard_map/kre,krc->kec/dot_general | solution.py:102
  23.4 5.0 %convolution_bitcast_fusion.1 = f32[1024,128]{1,0:T(8,128)S(1)} fusion(bf16[27,1024,128]{2,1,0:T(8,128)(2,1)} %fusion.14, bf16[27,128,128]{2,1,0:T(8,128)(2,1)S(1)} %copy-done.2), kind=kOutput, calls=%fused_computation.29 | convolution fusion | flops 905969664 | bytes 8486912 | tf_op jit(solution)/shard_map/ked,kcd->ec/dot_general | solution.py:114
  30.4 4.8 %collective-permute-start = (f32[256,128]{1,0:T(8,128)S(1)}, f32[256,128]{1,0:T(8,128)S(1)}, u32[]{:S(2)}, u32[]{:S(2)}) collective-permute-start(f32[256,128]{1,0:T(8,128)S(1)} %get-tuple-element.9), channel_id=1, source_target_pairs={{0,8},{8,16},{16,24},{24,32},{32,40},{40,48},{48,56},{56,64},{64,7... | collective-permute-start | bytes 393224 | tf_op jit(solution)/shard_map/ppermute | solution.py:12
  35.4 5.2 %fusion.3 = bf16[27,256,128]{2,1,0:T(8,128)(2,1)} fusion(s32[27,256]{1,0:T(8,128)S(1)} %get-tuple-element.23, bf16[256,128]{0,1:T(8,128)(2,1)S(1)} %collective-permute-done.3, bf16[256,128]{0,1:T(8,128)(2,1)S(1)} %collective-permute-done.2, bf16[512,128]{0,1:T(8,128)(2,1)S(1)} %bitcast_multiply_fusion.2), kind=kOutput, calls=%fused_computation.6 | convolution fusion | flops 1826881536 | bytes 2059264 | tf_op jit(solution)/shard_map/kre,ec->krc/dot_general | solution.py:102
  40.6 6.8 %fusion.22 = f32[512,128]{1,0:T(8,128)S(1)} fusion(bf16[27,128,128]{2,1,0:T(8,128)(2,1)S(1)} %copy-done, s32[27,256]{1,0:T(8,128)S(1)} %get-tuple-element.22, bf16[27,256,128]{2,1,0:T(8,128)(2,1)} %fusion.3), kind=kOutput, calls=%fused_computation.30 | convolution fusion | flops 1364262912 | bytes 2944000 | tf_op jit(solution)/shard_map/koc,kcd->od/dot_general | solution.py:106
  48.3 11.0 %fusion.15 = bf16[27,1024,128]{2,1,0:T(8,128)(2,1)} fusion(s32[27,256]{1,0:T(8,128)S(1)} %get-tuple-element.23, s32[27,256]{1,0:T(8,128)S(1)} %get-tuple-element.22, f32[512,128]{1,0:T(8,128)S(1)} %reshape.135, f32[1024,128]{1,0:T(8,128)S(1)} %convolution_bitcast_fusion.1, f32[512,128]{1,0:T(8,128)S(1)} %fusion.22, f32[512]{0:T(512)S(1)} %get-tuple-element.19), kind=kOutput, calls=%fused_computation.18 | convolution fusion | flops 2733670400 | bytes 7931904 | tf_op jit(solution)/shard_map/kre,krc->kec/dot_general | solution.py:102
  59.2 5.0 %convolution_bitcast_fusion = f32[1024,128]{1,0:T(8,128)S(1)} fusion(bf16[27,1024,128]{2,1,0:T(8,128)(2,1)} %fusion.15, bf16[27,128,128]{2,1,0:T(8,128)(2,1)S(1)} %copy-done), kind=kOutput, calls=%fused_computation.28 | convolution fusion | flops 905969664 | bytes 8486912 | tf_op jit(solution)/shard_map/ked,kcd->ec/dot_general | solution.py:114
  66.2 4.6 %collective-permute-start.4 = (f32[256,128]{1,0:T(8,128)S(1)}, f32[256,128]{1,0:T(8,128)S(1)}, u32[]{:S(2)}, u32[]{:S(2)}) collective-permute-start(f32[256,128]{1,0:T(8,128)S(1)} %get-tuple-element.7), channel_id=1, source_target_pairs={{0,8},{8,16},{16,24},{24,32},{32,40},{40,48},{48,56},{56,64},{64,7... | collective-permute-start | bytes 393224 | tf_op jit(solution)/shard_map/ppermute | solution.py:12
  76.9 5.0 %collective-permute-start.6 = (bf16[256,128]{1,0:T(8,128)(2,1)S(1)}, bf16[256,128]{1,0:T(8,128)(2,1)S(1)}, u32[]{:S(2)}, u32[]{:S(2)}) collective-permute-start(bf16[256,128]{1,0:T(8,128)(2,1)S(1)} %slice.87), channel_id=1, source_target_pairs={{0,8},{8,16},{16,24},{24,32},{32,40},{40,48},{48,56},{56,64},{64,7... | collective-permute-start | bytes 196616 | tf_op jit(solution)/shard_map/ppermute | solution.py:12
  81.9 4.1 %fusion.38 = f32[27,128,128]{1,2,0:T(8,128)S(1)} fusion(bf16[27,1024,128]{2,1,0:T(8,128)(2,1)} %fusion.15, bf16[256,128]{0,1:T(8,128)(2,1)S(1)} %collective-permute-done.3, bf16[256,128]{0,1:T(8,128)(2,1)S(1)} %collective-permute-done.2, bf16[512,128]{0,1:T(8,128)(2,1)S(1)} %bitcast_multiply_fusion.2), kind=kOutput, calls=%fused_computation.52 | convolution fusion | flops 906756096 | bytes 9109504 | tf_op jit(solution)/shard_map/ec,ked->kcd/dot_general | solution.py:115
  86.0 4.3 %broadcast_select_fusion.1 = (f32[27,128,128]{1,2,0:T(8,128)S(1)}, f32[27,128,128]{1,2,0:T(8,128)S(1)}) fusion(f32[27,128,128]{1,2,0:T(8,128)S(1)} %fusion.38, pred[]{:T(512)S(6)} %eq.69, bf16[27,1024,128]{2,1,0:T(8,128)(2,1)} %fusion.14, bf16[256,128]{1,0:T(8,128)(2,1)S(1)} %collective-permute-done.7, bf16[256,128]{1,0:T(8,128)(2,1)S(1)} %collective-permute-done.6, ...), kind=kOutput, calls=%fused_computation.32 | convolution fusion | flops 907640832 | bytes 12648449 | tf_op jit(solution)/shard_map/ec,ked->kcd/dot_general | solution.py:115
  90.3 3.4 %collective-permute-start.8 = (f32[3456,128]{1,0:T(8,128)S(1)}, f32[3456,128]{1,0:T(8,128)S(1)}, u32[]{:S(2)}, u32[]{:S(2)}) collective-permute-start(f32[3456,128]{1,0:T(8,128)S(1)} %bitcast.69), channel_id=1, source_target_pairs={{0,1},{1,0},{2,3},{3,2},{4,5},{5,4},{6,7},{7,6},{8,9},{9,8},{10,11... | collective-permute-start | bytes 5308424 | tf_op jit(solution)/shard_map/ppermute | solution.py:30
  93.7 3.3 %collective-permute-done.8 = f32[3456,128]{1,0:T(8,128)S(1)} collective-permute-done((f32[3456,128]{1,0:T(8,128)S(1)}, f32[3456,128]{1,0:T(8,128)S(1)}, u32[]{:S(2)}, u32[]{:S(2)}) %collective-permute-start.8) | collective-permute-done | bytes 1769504 | tf_op jit(solution)/shard_map/ppermute | solution.py:30
  98.6 12.0 %all-to-all-start = ((f32[32,108,128]{2,1,0:T(8,128)}), f32[32,108,128]{2,1,0:T(8,128)S(1)}, u32[]{:S(2)}, u32[]{:S(2)}) async-start(f32[32,108,128]{2,1,0:T(8,128)} %reshape.139), calls=%async_computation | async-start | bytes 3670016 | tf_op jit(solution)/shard_map/all_to_all | solution.py:46
  110.6 43.6 %all-to-all-done = f32[32,108,128]{2,1,0:T(8,128)S(1)} async-done(((f32[32,108,128]{2,1,0:T(8,128)}), f32[32,108,128]{2,1,0:T(8,128)S(1)}, u32[]{:S(2)}, u32[]{:S(2)}) %all-to-all-start) | async-done | bytes 1769504 | tf_op jit(solution)/shard_map/all_to_all | solution.py:46
  157.1 3.0 %collective-permute-start.10 = (f32[27,128]{1,0:T(8,128)S(1)}, f32[27,128]{1,0:T(8,128)S(1)}, u32[]{:S(2)}, u32[]{:S(2)}) collective-permute-start(f32[27,128]{1,0:T(8,128)S(1)} %slice_select_fusion.1), channel_id=1, source_target_pairs={{0,4},{1,5},{2,6},{3,7},{4,0},{5,1},{6,2},{7,3},{8,12},{9,13},{10,... | collective-permute-start | bytes 41480 | tf_op jit(solution)/shard_map/ppermute | solution.py:30
  161.3 2.9 %collective-permute-start.11 = (f32[27,128]{1,0:T(8,128)S(1)}, f32[27,128]{1,0:T(8,128)S(1)}, u32[]{:S(2)}, u32[]{:S(2)}) collective-permute-start(f32[27,128]{1,0:T(8,128)S(1)} %select_add_fusion.1), channel_id=1, source_target_pairs={{0,4},{1,5},{2,6},{3,7},{4,0},{5,1},{6,2},{7,3},{8,12},{9,13},{10,... | collective-permute-start | bytes 41480 | tf_op jit(solution)/shard_map/ppermute | solution.py:37
  168.4 44.9 %all_to_all.10 = f32[32,108,128]{2,1,0:T(8,128)S(1)} all-to-all(f32[32,108,128]{2,1,0:T(8,128)S(1)} %broadcast_in_dim.5), channel_id=1, replica_groups=mesh['space'=32,'dp'=8] {'space'}, dimensions={0} | all-to-all | bytes 3538944 | tf_op jit(solution)/shard_map/all_to_all | solution.py:52
  214.6 7.6 %collective-permute-start.13 = (f32[3456,128]{1,0:T(8,128)}, f32[3456,128]{1,0:T(8,128)S(1)}, u32[]{:S(2)}, u32[]{:S(2)}) collective-permute-start(f32[3456,128]{1,0:T(8,128)} %reshape.140), channel_id=1, source_target_pairs={{0,1},{1,0},{2,3},{3,2},{4,5},{5,4},{6,7},{7,6},{8,9},{9,8},{10,11... | collective-permute-start | bytes 5308424 | tf_op jit(solution)/shard_map/ppermute | solution.py:37
  222.3 3.5 %collective-permute-done.13 = f32[3456,128]{1,0:T(8,128)S(1)} collective-permute-done((f32[3456,128]{1,0:T(8,128)}, f32[3456,128]{1,0:T(8,128)S(1)}, u32[]{:S(2)}, u32[]{:S(2)}) %collective-permute-start.13) | collective-permute-done | bytes 1769504 | tf_op jit(solution)/shard_map/ppermute | solution.py:37
  225.8 2.5 %maximum_select_fusion = f32[6912,128]{1,0:T(8,128)S(1)} fusion(f32[3456,128]{1,0:T(8,128)} %reshape.140, f32[3456,128]{1,0:T(8,128)S(1)} %collective-permute-done.13, pred[]{:T(512)S(6)} %eq.69), kind=kLoop, calls=%fused_computation.19 | loop fusion | flops 2654208 | bytes 7077889 | tf_op jit(solution)/shard_map/jit(_where)/select_n | solution.py:38
  228.3 2.0 slice_multiply_fusion
  (65 shorter events, 27.3 us)
Async XLA Ops:
  0.6 39.9 %copy-start = (bf16[27,128,128]{2,1,0:T(8,128)(2,1)S(1)}, bf16[27,128,128]{2,1,0:T(8,128)(2,1)}, u32[]{:S(2)}) copy-start(bf16[27,128,128]{2,1,0:T(8,128)(2,1)} %param.9) | copy-start | bytes 2654212
  3.9 31.5 %collective-permute-start.3 = (bf16[256,128]{0,1:T(8,128)(2,1)S(1)}, bf16[256,128]{0,1:T(8,128)(2,1)S(1)}, u32[]{:S(2)}, u32[]{:S(2)}) collective-permute-start(bf16[256,128]{0,1:T(8,128)(2,1)S(1)} %copy.20), channel_id=1, source_target_pairs={{8,0},{16,8},{24,16},{32,24},{40,32},{48,40},{56,48},{64,56},{72,6... | collective-permute-start | bytes 196616 | tf_op jit(solution)/shard_map/ppermute | solution.py:15
  6.0 29.4 %collective-permute-start.2 = (bf16[256,128]{0,1:T(8,128)(2,1)S(1)}, bf16[256,128]{0,1:T(8,128)(2,1)S(1)}, u32[]{:S(2)}, u32[]{:S(2)}) collective-permute-start(bf16[256,128]{0,1:T(8,128)(2,1)S(1)} %copy.19), channel_id=1, source_target_pairs={{0,8},{8,16},{16,24},{24,32},{32,40},{40,48},{48,56},{56,64},{64,7... | collective-permute-start | bytes 196616 | tf_op jit(solution)/shard_map/ppermute | solution.py:12
  12.7 10.7 %copy-start.2 = (bf16[27,128,128]{2,1,0:T(8,128)(2,1)S(1)}, bf16[27,128,128]{2,1,0:T(8,128)(2,1)}, u32[]{:S(2)}) copy-start(bf16[27,128,128]{2,1,0:T(8,128)(2,1)} %param.10) | copy-start | bytes 2654212
  23.4 11.8 %copy-start.1 = (bf16[1,512,128]{2,1,0:T(8,128)(2,1)S(1)}, bf16[1,512,128]{2,1,0:T(8,128)(2,1)}, u32[]{:S(2)}) copy-start(bf16[1,512,128]{2,1,0:T(8,128)(2,1)} %param.7) | copy-start | bytes 393220
  28.5 18.9 %collective-permute-start.1 = (f32[256,128]{1,0:T(8,128)S(1)}, f32[256,128]{1,0:T(8,128)S(1)}, u32[]{:S(2)}, u32[]{:S(2)}) collective-permute-start(f32[256,128]{1,0:T(8,128)S(1)} %get-tuple-element.10), channel_id=1, source_target_pairs={{8,0},{16,8},{24,16},{32,24},{40,32},{48,40},{56,48},{64,56},{72,6... | collective-permute-start | bytes 393224 | tf_op jit(solution)/shard_map/ppermute | solution.py:15
  30.4 17.0 %collective-permute-start = (f32[256,128]{1,0:T(8,128)S(1)}, f32[256,128]{1,0:T(8,128)S(1)}, u32[]{:S(2)}, u32[]{:S(2)}) collective-permute-start(f32[256,128]{1,0:T(8,128)S(1)} %get-tuple-element.9), channel_id=1, source_target_pairs={{0,8},{8,16},{16,24},{24,32},{32,40},{40,48},{48,56},{56,64},{64,7... | collective-permute-start | bytes 393224 | tf_op jit(solution)/shard_map/ppermute | solution.py:12
  64.3 6.9 %collective-permute-start.5 = (f32[256,128]{1,0:T(8,128)S(1)}, f32[256,128]{1,0:T(8,128)S(1)}, u32[]{:S(2)}, u32[]{:S(2)}) collective-permute-start(f32[256,128]{1,0:T(8,128)S(1)} %get-tuple-element.8), channel_id=1, source_target_pairs={{8,0},{16,8},{24,16},{32,24},{40,32},{48,40},{56,48},{64,56},{72,6... | collective-permute-start | bytes 393224 | tf_op jit(solution)/shard_map/ppermute | solution.py:15
  66.2 6.5 %collective-permute-start.4 = (f32[256,128]{1,0:T(8,128)S(1)}, f32[256,128]{1,0:T(8,128)S(1)}, u32[]{:S(2)}, u32[]{:S(2)}) collective-permute-start(f32[256,128]{1,0:T(8,128)S(1)} %get-tuple-element.7), channel_id=1, source_target_pairs={{0,8},{8,16},{16,24},{24,32},{32,40},{40,48},{48,56},{56,64},{64,7... | collective-permute-start | bytes 393224 | tf_op jit(solution)/shard_map/ppermute | solution.py:12
  74.9 11.1 %collective-permute-start.7 = (bf16[256,128]{1,0:T(8,128)(2,1)S(1)}, bf16[256,128]{1,0:T(8,128)(2,1)S(1)}, u32[]{:S(2)}, u32[]{:S(2)}) collective-permute-start(bf16[256,128]{1,0:T(8,128)(2,1)S(1)} %slice.89), channel_id=1, source_target_pairs={{8,0},{16,8},{24,16},{32,24},{40,32},{48,40},{56,48},{64,56},{72,6... | collective-permute-start | bytes 196616 | tf_op jit(solution)/shard_map/ppermute | solution.py:15
  76.9 9.2 %collective-permute-start.6 = (bf16[256,128]{1,0:T(8,128)(2,1)S(1)}, bf16[256,128]{1,0:T(8,128)(2,1)S(1)}, u32[]{:S(2)}, u32[]{:S(2)}) collective-permute-start(bf16[256,128]{1,0:T(8,128)(2,1)S(1)} %slice.87), channel_id=1, source_target_pairs={{0,8},{8,16},{16,24},{24,32},{32,40},{40,48},{48,56},{56,64},{64,7... | collective-permute-start | bytes 196616 | tf_op jit(solution)/shard_map/ppermute | solution.py:12
  90.3 6.7 %collective-permute-start.8 = (f32[3456,128]{1,0:T(8,128)S(1)}, f32[3456,128]{1,0:T(8,128)S(1)}, u32[]{:S(2)}, u32[]{:S(2)}) collective-permute-start(f32[3456,128]{1,0:T(8,128)S(1)} %bitcast.69), channel_id=1, source_target_pairs={{0,1},{1,0},{2,3},{3,2},{4,5},{5,4},{6,7},{7,6},{8,9},{9,8},{10,11... | collective-permute-start | bytes 5308424 | tf_op jit(solution)/shard_map/ppermute | solution.py:30
  98.6 55.6 %all-to-all-start = ((f32[32,108,128]{2,1,0:T(8,128)}), f32[32,108,128]{2,1,0:T(8,128)S(1)}, u32[]{:S(2)}, u32[]{:S(2)}) async-start(f32[32,108,128]{2,1,0:T(8,128)} %reshape.139), calls=%async_computation | async-start | bytes 3670016 | tf_op jit(solution)/shard_map/all_to_all | solution.py:46
  154.3 2.8 %collective-permute-start.9 = (f32[54,128]{1,0:T(8,128)S(1)}, f32[54,128]{1,0:T(8,128)S(1)}, u32[]{:S(2)}, u32[]{:S(2)}) collective-permute-start(f32[54,128]{1,0:T(8,128)S(1)} %slice_select_fusion), channel_id=1, source_target_pairs={{0,2},{1,3},{2,0},{3,1},{4,6},{5,7},{6,4},{7,5},{8,10},{9,11},{10,... | collective-permute-start | bytes 82952 | tf_op jit(solution)/shard_map/ppermute | solution.py:30
  157.1 4.2 %collective-permute-start.10 = (f32[27,128]{1,0:T(8,128)S(1)}, f32[27,128]{1,0:T(8,128)S(1)}, u32[]{:S(2)}, u32[]{:S(2)}) collective-permute-start(f32[27,128]{1,0:T(8,128)S(1)} %slice_select_fusion.1), channel_id=1, source_target_pairs={{0,4},{1,5},{2,6},{3,7},{4,0},{5,1},{6,2},{7,3},{8,12},{9,13},{10,... | collective-permute-start | bytes 41480 | tf_op jit(solution)/shard_map/ppermute | solution.py:30
  161.3 4.1 %collective-permute-start.11 = (f32[27,128]{1,0:T(8,128)S(1)}, f32[27,128]{1,0:T(8,128)S(1)}, u32[]{:S(2)}, u32[]{:S(2)}) collective-permute-start(f32[27,128]{1,0:T(8,128)S(1)} %select_add_fusion.1), channel_id=1, source_target_pairs={{0,4},{1,5},{2,6},{3,7},{4,0},{5,1},{6,2},{7,3},{8,12},{9,13},{10,... | collective-permute-start | bytes 41480 | tf_op jit(solution)/shard_map/ppermute | solution.py:37
  165.4 2.8 %collective-permute-start.12 = (f32[54,128]{1,0:T(8,128)S(1)}, f32[54,128]{1,0:T(8,128)S(1)}, u32[]{:S(2)}, u32[]{:S(2)}) collective-permute-start(f32[54,128]{1,0:T(8,128)S(1)} %maximum_select_fusion.2), channel_id=1, source_target_pairs={{0,2},{1,3},{2,0},{3,1},{4,6},{5,7},{6,4},{7,5},{8,10},{9,11},{10,... | collective-permute-start | bytes 82952 | tf_op jit(solution)/shard_map/ppermute | solution.py:37
  214.6 11.2 %collective-permute-start.13 = (f32[3456,128]{1,0:T(8,128)}, f32[3456,128]{1,0:T(8,128)S(1)}, u32[]{:S(2)}, u32[]{:S(2)}) collective-permute-start(f32[3456,128]{1,0:T(8,128)} %reshape.140), channel_id=1, source_target_pairs={{0,1},{1,0},{2,3},{3,2},{4,5},{5,4},{6,7},{7,6},{8,9},{9,8},{10,11... | collective-permute-start | bytes 5308424 | tf_op jit(solution)/shard_map/ppermute | solution.py:37
